TPU v7x, 32 devices: a whole 2x2x4 slice. The times are simulated.
32 devices in a mesh: col: 8 (over y, x, core), row: 4 (over z).
Axes of the slice: x: 2, y: 2, z: 4, core: 2. Of those that a mesh axis runs over, the one named last changes fastest.
Arguments:
- p_blocks: bfloat16 [4, 72, 4096], P('row', 'col'), may hold values from -0.5390625 to 0.5390625
- p_slots: int32 [4, 72], P('row', 'col'), may hold values from 0 to 18, as said below
- out_slots: int32 [4, 104], P('row', 'col'), may hold values from 0 to 18, as said below
Outputs:
- purified: float32 [4, 104, 4096], P('row', 'col')
Inputs may be any that keep to these rules, and one draw needn't show every extreme that they name: `p_slots`: on each device the used slots (entries below 18) come first and name distinct positions; the remaining slots hold 18. Each device uses between half of its 9 slots (rounded up) and all of them, and some device uses all. `out_slots`: on each device the used slots (entries below 18) come first and name distinct positions; the remaining slots hold 18. Each device uses between half of its 13 slots (rounded up) and all of them, and some device uses all.
All inputs are finite; a program needn't handle non-finite values.
Results may differ from a plain program's by a relative error of at most 0.0003.
Values may be sent and summed in bfloat16 or wider, within the bound.
No kernel may reach another device: no remote copies, remote signals or barrier semaphores. Data moves between devices by JAX's collectives and lax.ppermute only.
A program may use at most 192 MiB of HBM per device.

v0:
```python
from functools import partial
import jax
import jax.numpy as jnp
from jax import lax
from jax.sharding import PartitionSpec as P

BLK = 64
COLS_DEV = 3


def add_terms(accum, portion, offset, table, capacity, rows_dev, block_edge, full_precision):
    block_vals, slot_ids = portion
    amount = slot_ids.shape[0]
    source = jnp.arange(amount, dtype=jnp.int32) // capacity
    local_row = slot_ids // COLS_DEV
    panel_row = source * COLS_DEV + slot_ids % COLS_DEV
    matching = table[panel_row]
    left = block_vals.reshape(amount, block_edge, block_edge)
    products = jnp.einsum("mab,mbw->maw", left, matching, preferred_element_type=jnp.float32)
    selector = (local_row[:, None] == jnp.arange(rows_dev, dtype=jnp.int32)[None, :]).astype(
        jnp.float32
    )
    return accum + jnp.einsum(
        "mr,maw->raw",
        selector,
        products,
        precision=lax.Precision.HIGHEST,
        preferred_element_type=jnp.float32,
    )


def on_device(p_blocks, p_slots, out_slots):
    n_row = lax.axis_size("row")
    n_col = lax.axis_size("col")
    capacity = p_slots.shape[1]
    block_edge = BLK
    rows_dev = COLS_DEV * n_col // n_row
    cells = rows_dev * COLS_DEV
    blocks_total = rows_dev * n_row
    width = COLS_DEV * block_edge
    own_blocks = p_blocks[0]
    own_ids = p_slots[0]
    down_blocks, down_ids = (
        lax.all_gather(own_blocks, "row", axis=0, tiled=True),
        lax.all_gather(own_ids, "row", axis=0, tiled=True),
    )
    source = jnp.arange(n_row * capacity, dtype=jnp.int32) // capacity
    panel_row = source * rows_dev + down_ids // COLS_DEV
    flat_index = jnp.where(
        down_ids < cells, panel_row * COLS_DEV + down_ids % COLS_DEV, blocks_total * COLS_DEV
    )
    column_panel = jnp.zeros((blocks_total * COLS_DEV, block_edge * block_edge), jnp.bfloat16)
    column_panel = column_panel.at[flat_index].set(down_blocks, mode="drop")
    column_panel = column_panel.reshape(blocks_total, COLS_DEV, block_edge, block_edge)
    column_panel = column_panel.transpose(0, 2, 1, 3).reshape(blocks_total, block_edge, width)
    empty = jnp.zeros((rows_dev, block_edge, width), jnp.float32)
    first_terms = partial(
        add_terms,
        table=column_panel,
        capacity=capacity,
        rows_dev=rows_dev,
        block_edge=block_edge,
        full_precision=False,
    )
    square = first_terms(
        empty,
        (
            lax.all_gather(own_blocks, "col", axis=0, tiled=True),
            lax.all_gather(own_ids, "col", axis=0, tiled=True),
        ),
        jnp.int32(0),
    )
    square_flat = square.reshape(rows_dev * block_edge, width)
    column_matrix = column_panel.reshape(blocks_total * block_edge, width).astype(jnp.float32)
    cube = jnp.dot(
        lax.all_gather(square_flat, "col", axis=1, tiled=True),
        column_matrix,
        precision=lax.Precision.HIGHEST,
        preferred_element_type=jnp.float32,
    )
    combined = 3.0 * square_flat - 2.0 * cube
    new_grid = combined.reshape(rows_dev, block_edge, COLS_DEV, block_edge).transpose(0, 2, 1, 3)
    new_grid = new_grid.reshape(cells, block_edge * block_edge)
    out_ids = out_slots[0]
    picked = new_grid[jnp.minimum(out_ids, cells - 1)]
    picked = jnp.where((out_ids < cells)[:, None], picked, jnp.zeros_like(picked))
    return picked[None]


def solution(mesh):
    in_specs = (P("row", "col", None), P("row", "col"), P("row", "col"))
    out_specs = P("row", "col", None)
    return jax.shard_map(
        on_device, mesh=mesh, in_specs=in_specs, out_specs=out_specs, check_vma=False
    )
```

profile of v0, /device:TPU:0, one launch (start us, length us, event | category | flops | bytes accessed | tf_op | source)
XLA Modules:
  0.0 116.2 jit_solution(5685451700651422301)
XLA Ops:
  6.5 0.0 all-gather.6.cloned.1.call-start
  6.5 1.1 copy.30
  7.6 18.3 %all-gather.2 = bf16[1,36,4096]{2,0,1:T(2,128)(2,1)S(1)} all-gather(bf16[1,9,4096]{2,0,1:T(2,128)(2,1)S(1)} %copy.30), channel_id=4, replica_groups=mesh['col'=8,'row'=4] {'row'}, dimensions={1}, use_global_device_ids=true | all-gather | bytes 368640 | tf_op jit(solution)/shard_map/all_gather | solution.py:44
  25.9 11.5 %all-gather.3 = bf16[1,72,4096]{2,0,1:T(2,128)(2,1)S(1)} all-gather(bf16[1,9,4096]{2,0,1:T(2,128)(2,1)S(1)} %copy.30), channel_id=5, replica_groups=mesh['col'=8,'row'=4] {'col'}, dimensions={1}, use_global_device_ids=true | all-gather | bytes 663552 | tf_op jit(solution)/shard_map/all_gather | solution.py:68
  37.4 0.0 copy-done.4
  37.4 0.7 dynamic-slice.1
  38.1 0.6 dynamic-slice
  40.0 0.0 copy-done.1
  40.0 0.1 bitcast_dynamic-update-slice_fusion.1
  40.1 7.0 %all-reduce = s32[72]{0:T(128)S(1)} all-reduce(s32[72]{0:T(128)S(1)} %get-tuple-element.7), channel_id=2, replica_groups=mesh['col'=8,'row'=4] {'col'}, use_global_device_ids=true, to_apply=%add | all-reduce | flops 72 | bytes 576
  47.2 8.0 %all-reduce.1 = s32[36]{0:T(128)S(1)} all-reduce(s32[36]{0:T(128)S(1)} %get-tuple-element.8), channel_id=3, replica_groups=mesh['col'=8,'row'=4] {'row'}, use_global_device_ids=true, to_apply=%add.1 | all-reduce | flops 36 | bytes 288
  55.2 1.5 %scatter_custom_fusion = bf16[72,4096]{1,0:T(8,128)(2,1)S(1)} fusion(s32[36]{0:T(128)S(1)} %compare_select_fusion.2, bf16[1,36,4096]{2,0,1:T(2,128)(2,1)S(1)} %all-gather.2, bf16[]{:T(256)} %constant.56.clone.1), kind=kCustom, calls=%fused_computation.8 | custom fusion | bytes 1179650 | tf_op jit(solution)/shard_map/scatter | solution.py:53
  56.7 1.3 %reshape.73 = bf16[24,3,64,64]{3,2,1,0:T(8,128)(2,1)S(1)} reshape(bf16[72,4096]{1,0:T(8,128)(2,1)S(1)} %scatter_custom_fusion) | data formatting | bytes 1179648 | tf_op jit(solution)/shard_map/reshape | solution.py:54
  58.0 3.6 %reduce = bf16[72,4096]{1,0:T(8,128)(2,1)S(1)} reduce(bf16[1,72,4096]{2,0,1:T(2,128)(2,1)S(1)} %all-gather.3, bf16[]{:T(256)} %constant.80), dimensions={0}, to_apply=%all-gather.3.reduce_sub_computation | reduce | bytes 1179650 | tf_op jit(solution)/shard_map/all_gather | solution.py:68
  61.5 1.3 %reshape.75 = bf16[72,64,64]{2,1,0:T(8,128)(2,1)S(1)} reshape(bf16[72,4096]{1,0:T(8,128)(2,1)S(1)} %reduce) | data formatting | bytes 1179648 | tf_op jit(solution)/shard_map/reshape | solution.py:18
  62.8 0.9 copy.31
  63.7 3.0 %gather_fusion = bf16[72,64,192]{1,2,0:T(8,128)(2,1)} fusion(bf16[24,64,192]{1,2,0:T(8,128)(2,1)S(1)} %bitcast.40, s32[1024]{0:T(1024)S(1)} %pad_clamp_fusion.1), kind=kCustom, calls=%fused_computation | custom fusion | bytes 3539232 | tf_op jit(solution)/shard_map/gather | solution.py:17
  66.7 4.4 %convolution_bitcast_fusion = f32[72,64,192]{2,1,0:T(8,128)S(1)} fusion(bf16[72,64,192]{1,2,0:T(8,128)(2,1)} %gather_fusion, bf16[72,64,64]{2,1,0:T(8,128)(2,1)S(1)} %reshape.75), kind=kOutput, calls=%fused_computation.5 | convolution fusion | flops 113246208 | bytes 5898240 | tf_op jit(solution)/shard_map/mab,mbw->maw/dot_general | solution.py:19
  71.1 4.3 %fusion = f32[6,64,192]{2,0,1:T(8,128)S(1)} fusion(f32[72,64,192]{2,1,0:T(8,128)S(1)} %convolution_bitcast_fusion, s32[72]{0:T(128)S(1)} %get-tuple-element.5), kind=kOutput, calls=%fused_computation.3 | convolution fusion | flops 63701424 | bytes 3834144 | tf_op jit(solution)/shard_map/mr,maw->raw/dot_general | solution.py:23
  75.4 0.1 copy.35
  75.5 0.9 copy.36
  76.4 0.0 all-gather.6.cloned.1.call-update
  76.4 1.3 %copy.38 = bf16[24,64,3,64]{1,0,3,2:T(8,128)(2,1)S(1)} copy(bf16[24,64,3,64]{3,1,2,0:T(8,128)(2,1)S(1)} %bitcast.39) | data formatting | bytes 1179648 | tf_op jit(solution)/shard_map/transpose | solution.py:55
  77.8 0.7 reshape_reshape.3
  78.5 25.6 %all-gather.6.cloned.1.call-done = f32[384,1536]{0,1:T(8,128)} async-done(((f32[384,192]{0,1:T(8,128)}), f32[384,1536]{0,1:T(8,128)}) %all-gather.6.cloned.1.call-update) | async-done | bytes 2359312 | tf_op jit(solution)/shard_map/all_gather | solution.py:76
  104.1 2.9 %fusion.2 = f32[384,192]{0,1:T(8,128)S(1)} fusion(f32[384,1536]{0,1:T(8,128)} %all-gather.6.cloned.1.call-done, bf16[1536,192]{0,1:T(8,128)(2,1)S(1)} %reshape_reshape.3, f32[384,192]{0,1:T(8,128)S(1)} %copy-done), kind=kOutput, calls=%fused_computation.7 | convolution fusion | flops 1359175680 | bytes 3538944 | tf_op jit(solution)/shard_map/dot_general | solution.py:75
  107.1 0.2 reshape.77
  107.3 0.3 copy.39
  107.5 0.2 reshape.78
  107.7 0.6 gather_fusion.1
  108.4 0.1 bitcast_select_fusion
  108.5 0.9 copy.40
  (16 shorter events, 0.1 us)
Async XLA Ops:
  6.5 30.9 %copy-start.4 = (u32[32]{0:T(128)S(1)}, u32[32]{0:T(128)}, u32[]{:S(2)}) copy-start(u32[32]{0:T(128)} %constant.75) | copy-start | bytes 388
  6.5 31.5 %copy-start.3 = (u32[32]{0:T(128)S(1)}, u32[32]{0:T(128)}, u32[]{:S(2)}) copy-start(u32[32]{0:T(128)} %constant.70) | copy-start | bytes 388
  6.5 33.5 %copy-start.1 = (s32[1,9]{1,0:T(1,128)S(1)}, s32[1,9]{1,0:T(1,128)}, u32[]{:S(2)}) copy-start(s32[1,9]{1,0:T(1,128)} %param.4) | copy-start | bytes 112
  6.5 97.6 %all-gather.6.cloned.1.call-start = ((), (), s32[]{:S(2)}) async-start(), calls=%async_computation | async-start | bytes 2654208 | tf_op jit(solution)/shard_map/all_gather | solution.py:76
  76.4 2.1 %copy-start.2 = (s32[1,13]{1,0:T(1,128)S(1)}, s32[1,13]{1,0:T(1,128)}, u32[]{:S(2)}) copy-start(s32[1,13]{1,0:T(1,128)} %param.5) | copy-start | bytes 160
  76.4 27.7 %copy-start = (f32[384,192]{0,1:T(8,128)S(1)}, f32[384,192]{0,1:T(8,128)}, u32[]{:S(2)}) copy-start(f32[384,192]{0,1:T(8,128)} %copy.36) | copy-start | bytes 884740
Sparse Core Ops, SparseCore 0:
  76.5 27.5 all-gather.5
where the time goes:
time: 116 us
  blocking collectives  44.8 us (39%)
  waiting for transfers between devices  25.6 us (22%)
  local copies, waits for them, and re-layouts  15.6 us (13%)
  between operations  14.9 us (13%)
  matrix products  11.6 us (10%)
  other arithmetic  3.71 us (3%)
    all_gather x1, waiting for transfers between devices, on_device(): lax.all_gather(square_flat, 'col', axis=1, tiled=True)  25.6 us
    all_gather x1, blocking collectives, on_device(): lax.all_gather(own_blocks, 'row', axis=0, tiled=True)  18.3 us
    unnamed x2, blocking collectives  15 us
    all_gather x1, blocking collectives, on_device(): lax.all_gather(own_blocks, 'col', axis=0, tiled=True)  11.5 us
    dot_general x1, matrix products, add_terms(): jnp.einsum('mab,mbw->maw', left, matching, preferred_element_type=jnp.flo...  4.36 us
    dot_general x1, matrix products, add_terms(): jnp.einsum('mr,maw->raw', selector, products, precision=lax.Precision.HIG...  4.29 us
    all_gather x1, other arithmetic, on_device(): lax.all_gather(own_blocks, 'col', axis=0, tiled=True)  3.56 us
    gather x1, local copies, waits for them, and re-layouts, add_terms(): matching = table[panel_row]  3.03 us
  transfers between devices with their start and end apart: 1, of which 1 were waited for; matrix products, arithmetic and copies ran while one was open for 2% of the time, Pallas kernels for 0%

commit v1 on v0

--- a/solution.py
+++ b/solution.py
@@ -6,6 +6,27 @@
 
 BLK = 64
 COLS_DEV = 3
+
+
+def ring_gather(shard, axis, dim):
+    size, mine, rows = (lax.axis_size(axis), lax.axis_index(axis), shard.shape[dim])
+    forward = [(i, (i + 1) % size) for i in range(size)]
+    behind = [(i, (i - 1) % size) for i in range(size)]
+    filled = jnp.zeros((*shard.shape[:dim], size * rows, *shard.shape[dim + 1 :]), shard.dtype)
+    filled = lax.dynamic_update_slice_in_dim(filled, shard, mine * rows, axis=dim)
+    from_left = from_right = shard
+    half = size // 2
+    for hop in range(1, half + 1):
+        from_left = lax.ppermute(from_left, axis, forward)
+        filled = lax.dynamic_update_slice_in_dim(
+            filled, from_left, (mine - hop) % size * rows, axis=dim
+        )
+        if hop < size - half:
+            from_right = lax.ppermute(from_right, axis, behind)
+            filled = lax.dynamic_update_slice_in_dim(
+                filled, from_right, (mine + hop) % size * rows, axis=dim
+            )
+    return filled
 
 
 def add_terms(accum, portion, offset, table, capacity, rows_dev, block_edge, full_precision):
@@ -64,10 +85,7 @@
     )
     square = first_terms(
         empty,
-        (
-            lax.all_gather(own_blocks, "col", axis=0, tiled=True),
-            lax.all_gather(own_ids, "col", axis=0, tiled=True),
-        ),
+        (ring_gather(own_blocks, "col", 0), lax.all_gather(own_ids, "col", axis=0, tiled=True)),
         jnp.int32(0),
     )
     square_flat = square.reshape(rows_dev * block_edge, width)

time: 116 us -> 123 us (1.060)
  local copies, waits for them, and re-layouts: 15.6 us -> 27.8 us
  blocking collectives: 44.8 us -> 32.8 us
  starting transfers between devices: 0.01 us -> 6.61 us
  other arithmetic: 3.71 us -> 0.15 us
  waiting for transfers between devices: 25.6 us -> 28.3 us
    all_gather x1 -> x0, blocking collectives: 11.5 us -> none  [on_device(): lax.all_gather(own_blocks, 'col', axis=0, tiled=True)]
    dynamic_update_slice x0 -> x8, local copies, waits for them, and re-layouts: none -> 10.5 us  [the longest x3 4.76 us: ring_gather(): lax.dynamic_update_slice_in_dim(filled, from_right, (mine + hop) % size *...]
    ppermute x0 -> x7, starting transfers between devices: none -> 6.61 us  [the longest x3 6.11 us: ring_gather(): from_right = lax.ppermute(from_right, axis, behind)]
    all_gather x1 -> x0, other arithmetic: 3.56 us -> none  [on_device(): lax.all_gather(own_blocks, 'col', axis=0, tiled=True)]
    all_gather x1, blocking collectives: 18.3 us -> 16.2 us  [on_device(): lax.all_gather(own_blocks, 'row', axis=0, tiled=True)]
    unnamed x16 -> x12, local copies, waits for them, and re-layouts: 2.44 us -> 4.27 us
    ppermute x0 -> x7, waiting for transfers between devices: none -> 1.82 us  [the longest x4 1.82 us: ring_gather(): from_left = lax.ppermute(from_left, axis, forward)]
    unnamed x2, blocking collectives: 15 us -> 16.6 us
  transfers between devices with their start and end apart: 1 -> 8, of which waited for: 1 -> 2; matrix products, arithmetic and copies ran while one was open for 2% -> 18% of each run, Pallas kernels for 0% -> 0%
where the time goes in v1:
time: 123 us; the launch traced here: 122 us
  blocking collectives  32.8 us (27%)
  waiting for transfers between devices  28.3 us (23%)
  local copies, waits for them, and re-layouts  27.8 us (23%)
  between operations  15 us (12%)
  matrix products  11.6 us (9%)
  starting transfers between devices  6.61 us (5%)
    all_gather x1, waiting for transfers between devices, on_device(): lax.all_gather(square_flat, 'col', axis=1, tiled=True)  26.5 us
    unnamed x2, blocking collectives  16.6 us
    all_gather x1, blocking collectives, on_device(): lax.all_gather(own_blocks, 'row', axis=0, tiled=True)  16.2 us
    ppermute x3, starting transfers between devices, ring_gather(): from_right = lax.ppermute(from_right, axis, behind)  6.11 us
    dynamic_update_slice x3, local copies, waits for them, and re-layouts, ring_gather(): lax.dynamic_update_slice_in_dim(filled, from_right, (mine + hop) % size *...  4.76 us
    dynamic_update_slice x4, local copies, waits for them, and re-layouts, ring_gather(): lax.dynamic_update_slice_in_dim(filled, from_left, (mine - hop) % size *...  4.61 us
    dot_general x1, matrix products, add_terms(): jnp.einsum('mab,mbw->maw', left, matching, preferred_element_type=jnp.flo...  4.37 us
    dot_general x1, matrix products, add_terms(): jnp.einsum('mr,maw->raw', selector, products, precision=lax.Precision.HIG...  4.28 us
  transfers between devices with their start and end apart: 8, of which 2 were waited for; matrix products, arithmetic and copies ran while one was open for 18% of the time, Pallas kernels for 0%

profile of v1, /device:TPU:0, one launch (start us, length us, event | category | flops | bytes accessed | tf_op | source)
XLA Modules:
  0.0 122.2 jit_solution(5937367066940981621)
XLA Ops:
  6.5 3.4 %collective-permute-start.1 = (bf16[9,4096]{1,0:T(8,128)(2,1)}, bf16[9,4096]{1,0:T(8,128)(2,1)S(1)}, u32[]{:S(2)}, u32[]{:S(2)}) collective-permute-start(bf16[9,4096]{1,0:T(8,128)(2,1)} %bitcast.42), channel_id=1, source_target_pairs={{0,28},{4,0},{8,4},{12,8},{16,12},{20,16},{24,20},{28,24},{1,29},{... | collective-permute-start | bytes 221192 | tf_op jit(solution)/shard_map/ppermute | solution.py:25
  9.9 1.2 %dynamic-slice.1 = u32[1]{0:T(128)} dynamic-slice(u32[32]{0:T(128)} %constant.129, u32[]{:T(128)S(6)} %add.131), dynamic_slice_sizes={1} | dynamic-slice | bytes 12
  11.1 1.2 %dynamic-slice = u32[1]{0:T(128)} dynamic-slice(u32[32]{0:T(128)} %constant.124, u32[]{:T(128)S(6)} %add.131), dynamic_slice_sizes={1} | dynamic-slice | bytes 12
  13.6 0.8 bitcast_dynamic-update-slice_fusion.1
  14.4 8.1 %all-reduce = s32[72]{0:T(128)S(1)} all-reduce(s32[72]{0:T(128)S(1)} %get-tuple-element.7), channel_id=2, replica_groups=mesh['col'=8,'row'=4] {'col'}, use_global_device_ids=true, to_apply=%add | all-reduce | flops 72 | bytes 576
  22.5 8.5 %all-reduce.1 = s32[36]{0:T(128)S(1)} all-reduce(s32[36]{0:T(128)S(1)} %get-tuple-element.8), channel_id=3, replica_groups=mesh['col'=8,'row'=4] {'row'}, use_global_device_ids=true, to_apply=%add.1 | all-reduce | flops 36 | bytes 288
  31.1 1.0 copy.29
  32.2 2.7 %collective-permute-start.3 = (bf16[9,4096]{1,0:T(8,128)(2,1)S(1)}, bf16[9,4096]{1,0:T(8,128)(2,1)}, u32[]{:S(2)}, u32[]{:S(2)}) collective-permute-start(bf16[9,4096]{1,0:T(8,128)(2,1)S(1)} %collective-permute-done.1), channel_id=1, source_target_pairs={{0,28},{4,0},{8,4},{12,8},{16,12},{20,16},{24,20},{28,24},{1,29},{... | collective-permute-start | bytes 221192 | tf_op jit(solution)/shard_map/ppermute | solution.py:25
  34.9 1.8 %collective-permute-done.2 = bf16[9,4096]{1,0:T(8,128)(2,1)S(1)} collective-permute-done((bf16[9,4096]{1,0:T(8,128)(2,1)S(1)}, bf16[9,4096]{1,0:T(8,128)(2,1)S(1)}, u32[]{:S(2)}, u32[]{:S(2)}) %collective-permute-start.2) | collective-permute-done | bytes 73760 | tf_op jit(solution)/shard_map/ppermute | solution.py:20
  36.7 16.2 %all-gather.2 = bf16[1,36,4096]{2,0,1:T(2,128)(2,1)S(1)} all-gather(bf16[1,9,4096]{2,0,1:T(2,128)(2,1)S(1)} %copy.29), channel_id=4, replica_groups=mesh['col'=8,'row'=4] {'row'}, dimensions={1}, use_global_device_ids=true | all-gather | bytes 368640 | tf_op jit(solution)/shard_map/all_gather | solution.py:65
  52.8 1.5 %scatter_custom_fusion = bf16[72,4096]{1,0:T(8,128)(2,1)S(1)} fusion(s32[36]{0:T(128)S(1)} %compare_select_fusion.2, bf16[1,36,4096]{2,0,1:T(2,128)(2,1)S(1)} %all-gather.2, bf16[]{:T(256)} %constant.102.clone.1), kind=kCustom, calls=%fused_computation.7 | custom fusion | bytes 1179650 | tf_op jit(solution)/shard_map/scatter | solution.py:74
  54.4 1.3 %reshape.74 = bf16[24,3,64,64]{3,2,1,0:T(8,128)(2,1)S(1)} reshape(bf16[72,4096]{1,0:T(8,128)(2,1)S(1)} %scatter_custom_fusion) | data formatting | bytes 1179648 | tf_op jit(solution)/shard_map/reshape | solution.py:75
  55.6 0.7 copy.30
  56.5 1.2 dynamic_update_slice.24
  58.2 3.0 %gather_fusion = bf16[72,64,192]{1,2,0:T(8,128)(2,1)} fusion(bf16[24,64,192]{1,2,0:T(8,128)(2,1)S(1)} %bitcast.39, s32[1024]{0:T(1024)S(1)} %pad_clamp_fusion.1), kind=kCustom, calls=%fused_computation | custom fusion | bytes 3539232 | tf_op jit(solution)/shard_map/gather | solution.py:38
  61.2 0.7 dynamic_update_slice.25
  61.9 1.2 dynamic_update_slice.26
  63.1 1.0 dynamic_update_slice.27
  64.1 1.8 %dynamic_update_slice.28 = bf16[72,4096]{1,0:T(8,128)(2,1)S(1)} dynamic-update-slice(bf16[72,4096]{1,0:T(8,128)(2,1)S(1)} %dynamic_update_slice.27, bf16[9,4096]{1,0:T(8,128)(2,1)} %collective-permute-done.3, s32[]{:T(128)S(6)} %select_n.123, s32[]{:T(128)} %constant.100.clone.1) | dynamic-update-slice | bytes 147460 | tf_op jit(solution)/shard_map/dynamic_update_slice | solution.py:26
  65.9 1.8 %dynamic_update_slice.29 = bf16[72,4096]{1,0:T(8,128)(2,1)S(1)} dynamic-update-slice(bf16[72,4096]{1,0:T(8,128)(2,1)S(1)} %dynamic_update_slice.28, bf16[9,4096]{1,0:T(8,128)(2,1)} %collective-permute-done.4, s32[]{:T(128)S(6)} %select_n.125, s32[]{:T(128)} %constant.100.clone.1) | dynamic-update-slice | bytes 147460 | tf_op jit(solution)/shard_map/dynamic_update_slice | solution.py:21
  67.7 1.8 %dynamic_update_slice.30 = bf16[72,4096]{1,0:T(8,128)(2,1)S(1)} dynamic-update-slice(bf16[72,4096]{1,0:T(8,128)(2,1)S(1)} %dynamic_update_slice.29, bf16[9,4096]{1,0:T(8,128)(2,1)} %collective-permute-done.5, s32[]{:T(128)S(6)} %select_n.127, s32[]{:T(128)} %constant.100.clone.1) | dynamic-update-slice | bytes 147460 | tf_op jit(solution)/shard_map/dynamic_update_slice | solution.py:26
  69.5 1.2 dynamic_update_slice.31
  70.7 1.3 %reshape.73 = bf16[72,64,64]{2,1,0:T(8,128)(2,1)S(1)} reshape(bf16[72,4096]{1,0:T(8,128)(2,1)S(1)} %dynamic_update_slice.31) | data formatting | bytes 1179648 | tf_op jit(solution)/shard_map/reshape | solution.py:39
  71.9 4.4 %fusion.19 = f32[72,64,192]{2,1,0:T(8,128)S(1)} fusion(bf16[72,64,64]{2,1,0:T(8,128)(2,1)S(1)} %reshape.73, bf16[72,64,192]{1,2,0:T(8,128)(2,1)} %gather_fusion), kind=kOutput, calls=%fused_computation.45 | convolution fusion | flops 113246208 | bytes 5898240 | tf_op jit(solution)/shard_map/mab,mbw->maw/dot_general | solution.py:40
  76.3 4.3 %fusion = f32[6,64,192]{2,0,1:T(8,128)S(1)} fusion(f32[72,64,192]{2,1,0:T(8,128)S(1)} %fusion.19, s32[72]{0:T(128)S(1)} %get-tuple-element.5), kind=kOutput, calls=%fused_computation.3 | convolution fusion | flops 63701424 | bytes 3834144 | tf_op jit(solution)/shard_map/mr,maw->raw/dot_general | solution.py:44
  80.7 0.9 copy.34
  81.6 1.3 %copy.36 = bf16[24,64,3,64]{1,0,3,2:T(8,128)(2,1)S(1)} copy(bf16[24,64,3,64]{3,1,2,0:T(8,128)(2,1)S(1)} %bitcast.38) | data formatting | bytes 1179648 | tf_op jit(solution)/shard_map/transpose | solution.py:76
  82.9 0.7 reshape_reshape.3
  83.7 26.5 %all-gather.5.cloned.1.call-done = f32[384,1536]{0,1:T(8,128)} async-done(((f32[384,192]{0,1:T(8,128)}), f32[384,1536]{0,1:T(8,128)}) %all-gather.5.cloned.1.call-update) | async-done | bytes 2359312 | tf_op jit(solution)/shard_map/all_gather | solution.py:94
  110.2 2.9 %fusion.2 = f32[384,192]{0,1:T(8,128)S(1)} fusion(f32[384,1536]{0,1:T(8,128)} %all-gather.5.cloned.1.call-done, bf16[1536,192]{0,1:T(8,128)(2,1)S(1)} %reshape_reshape.3, f32[384,192]{0,1:T(8,128)S(1)} %copy-done), kind=kOutput, calls=%fused_computation.6 | convolution fusion | flops 1359175680 | bytes 3538944 | tf_op jit(solution)/shard_map/dot_general | solution.py:93
  113.8 0.6 gather_fusion.1
  114.5 0.9 copy.38
  (33 shorter events, 1.6 us)
Async XLA Ops:
  6.5 103.6 %all-gather.5.cloned.1.call-start = ((), (), s32[]{:S(2)}) async-start(), calls=%async_computation | async-start | bytes 2654208 | tf_op jit(solution)/shard_map/all_gather | solution.py:94
  6.5 25.6 %collective-permute-start.1 = (bf16[9,4096]{1,0:T(8,128)(2,1)}, bf16[9,4096]{1,0:T(8,128)(2,1)S(1)}, u32[]{:S(2)}, u32[]{:S(2)}) collective-permute-start(bf16[9,4096]{1,0:T(8,128)(2,1)} %bitcast.42), channel_id=1, source_target_pairs={{0,28},{4,0},{8,4},{12,8},{16,12},{20,16},{24,20},{28,24},{1,29},{... | collective-permute-start | bytes 221192 | tf_op jit(solution)/shard_map/ppermute | solution.py:25
  9.9 21.1 %collective-permute-start = (bf16[9,4096]{1,0:T(8,128)(2,1)}, bf16[9,4096]{1,0:T(8,128)(2,1)S(1)}, u32[]{:S(2)}, u32[]{:S(2)}) collective-permute-start(bf16[9,4096]{1,0:T(8,128)(2,1)} %bitcast.43), channel_id=1, source_target_pairs={{0,4},{4,8},{8,12},{12,16},{16,20},{20,24},{24,28},{28,0},{1,5},{5... | collective-permute-start | bytes 221192 | tf_op jit(solution)/shard_map/ppermute | solution.py:20
  31.0 5.7 %collective-permute-start.2 = (bf16[9,4096]{1,0:T(8,128)(2,1)S(1)}, bf16[9,4096]{1,0:T(8,128)(2,1)S(1)}, u32[]{:S(2)}, u32[]{:S(2)}) collective-permute-start(bf16[9,4096]{1,0:T(8,128)(2,1)S(1)} %collective-permute-done), channel_id=1, source_target_pairs={{0,4},{4,8},{8,12},{12,16},{16,20},{20,24},{24,28},{28,0},{1,5},{5... | collective-permute-start | bytes 221192 | tf_op jit(solution)/shard_map/ppermute | solution.py:20
  32.2 25.4 %collective-permute-start.3 = (bf16[9,4096]{1,0:T(8,128)(2,1)S(1)}, bf16[9,4096]{1,0:T(8,128)(2,1)}, u32[]{:S(2)}, u32[]{:S(2)}) collective-permute-start(bf16[9,4096]{1,0:T(8,128)(2,1)S(1)} %collective-permute-done.1), channel_id=1, source_target_pairs={{0,28},{4,0},{8,4},{12,8},{16,12},{20,16},{24,20},{28,24},{1,29},{... | collective-permute-start | bytes 221192 | tf_op jit(solution)/shard_map/ppermute | solution.py:25
  36.7 21.0 %collective-permute-start.4 = (bf16[9,4096]{1,0:T(8,128)(2,1)S(1)}, bf16[9,4096]{1,0:T(8,128)(2,1)}, u32[]{:S(2)}, u32[]{:S(2)}) collective-permute-start(bf16[9,4096]{1,0:T(8,128)(2,1)S(1)} %collective-permute-done.2), channel_id=1, source_target_pairs={{0,4},{4,8},{8,12},{12,16},{16,20},{20,24},{24,28},{28,0},{1,5},{5... | collective-permute-start | bytes 221192 | tf_op jit(solution)/shard_map/ppermute | solution.py:20
  54.3 2.1 %copy-start.1 = (bf16[1,9,4096]{2,1,0:T(8,128)(2,1)S(1)}, bf16[1,9,4096]{2,1,0:T(8,128)(2,1)}, u32[]{:S(2)}) copy-start(bf16[1,9,4096]{2,1,0:T(8,128)(2,1)} %param.3) | copy-start | bytes 221188
  57.6 10.0 %collective-permute-start.5 = (bf16[9,4096]{1,0:T(8,128)(2,1)}, bf16[9,4096]{1,0:T(8,128)(2,1)}, u32[]{:S(2)}, u32[]{:S(2)}) collective-permute-start(bf16[9,4096]{1,0:T(8,128)(2,1)} %collective-permute-done.3), channel_id=1, source_target_pairs={{0,28},{4,0},{8,4},{12,8},{16,12},{20,16},{24,20},{28,24},{1,29},{... | collective-permute-start | bytes 221192 | tf_op jit(solution)/shard_map/ppermute | solution.py:25
  57.7 11.8 %collective-permute-start.6 = (bf16[9,4096]{1,0:T(8,128)(2,1)}, bf16[9,4096]{1,0:T(8,128)(2,1)S(1)}, u32[]{:S(2)}, u32[]{:S(2)}) collective-permute-start(bf16[9,4096]{1,0:T(8,128)(2,1)} %collective-permute-done.4), channel_id=1, source_target_pairs={{0,4},{4,8},{8,12},{12,16},{16,20},{20,24},{24,28},{28,0},{1,5},{5... | collective-permute-start | bytes 221192 | tf_op jit(solution)/shard_map/ppermute | solution.py:20
  81.6 2.1 %copy-start.2 = (s32[1,13]{1,0:T(1,128)S(1)}, s32[1,13]{1,0:T(1,128)}, u32[]{:S(2)}) copy-start(s32[1,13]{1,0:T(1,128)} %param.5) | copy-start | bytes 160
  81.6 28.6 %copy-start = (f32[384,192]{0,1:T(8,128)S(1)}, f32[384,192]{0,1:T(8,128)}, u32[]{:S(2)}) copy-start(f32[384,192]{0,1:T(8,128)} %copy.34) | copy-start | bytes 884740
Sparse Core Ops, SparseCore 0:
  81.7 28.3 all-gather.4
